TPU v7x, 32 devices: a whole 2x2x4 slice. The times are simulated.
32 devices in a mesh: req: 8 (over y, x, core), tp: 4 (over z).
Axes of the slice: x: 2, y: 2, z: 4, core: 2. Of those that a mesh axis runs over, the one named last changes fastest.
Arguments:
- queries: bfloat16 [1536, 2560], P('req', 'tp'), may hold values from -5 to 5
- new_keys: bfloat16 [1536, 512], P('req', 'tp'), may hold values from -5 to 5
- new_values: bfloat16 [1536, 512], P('req', 'tp'), may hold values from -5 to 5
- key_pages: bfloat16 [512, 64, 512], P('req', None, 'tp'), may hold values from -5 to 5
- value_pages: bfloat16 [512, 64, 512], P('req', None, 'tp'), may hold values from -5 to 5
- page_table: int32 [32, 16], P('req'), may hold values from 0 to 511, as said below
- cache_lengths: int32 [32], P('req'), may hold values from 2 to 1024, as said below
- parents: int32 [32, 48], P('req'), may hold values from -1 to 46, as said below
- residual: bfloat16 [1536, 2560], P('req'), may hold values from -6 to 6
- out_weight: bfloat16 [2560, 2560], P('tp'), may hold values from -0.125 to 0.125
- norm_gain: float32 [2560], replicated, may hold values from 0.1 to 1.9
- router_weight: float32 [2560, 16], replicated, may hold values from -0.125 to 0.125
- routes: int32 [1536, 6], P('req'), may hold values from 0 to 15, all different within a row; in each aligned block of 192 rows (0 to 191, 192 to 383, ...) at most 91 rows name the same one
- expert_gate_up: bfloat16 [16, 2560, 2, 1536], P('req', None, None, 'tp'), may hold values from -0.125 to 0.125
- expert_down: bfloat16 [16, 1536, 2560], P('req', 'tp'), may hold values from -0.15625 to 0.15625
- shared_gate_up: bfloat16 [2560, 2, 1536], P(None, None, 'tp'), may hold values from -0.125 to 0.125
- shared_down: bfloat16 [1536, 2560], P('tp'), may hold values from -0.15625 to 0.15625
Outputs:
- layer_out: bfloat16 [1536, 2560], P('req', 'tp')
Inputs may be any that keep to these rules, and one draw needn't show every extreme that they name: `page_table`: the pages of the 4 requests of the d-th block of 4 rows are the d-th block of 64 pages of the pool, each named once. `cache_lengths`: some request holds 1024 positions. parents[r, 0] = -1, and 0 <= parents[r, i] < i for i >= 1. `routes`: A token's 6 experts differ. In each aligned block of 192 rows no expert is named by more than 91 rows, and in some block one expert is named by exactly 91.
All inputs are finite; a program needn't handle non-finite values.
Results may differ from a plain program's by a relative error of at most 0.02.
Values may be sent and summed in bfloat16 or wider, within the bound.
No kernel may reach another device: no remote copies, remote signals or barrier semaphores. Data moves between devices by JAX's collectives and lax.ppermute only.
A program may use at most 128 MiB of HBM per device.

v0:
```python
import math
import jax
import jax.numpy as jnp
from jax import lax
from jax.sharding import PartitionSpec as P

QH = 20
KVH = 4
HD = 128
EPSILON = 1e-06
NEGATIVE = -1e30


def rounded(values):
    return lax.optimization_barrier(values.astype(jnp.bfloat16)).astype(jnp.float32)


def ancestors(parents):
    tree_size = parents.shape[-1]
    position = jnp.arange(tree_size, dtype=jnp.int32)
    adjacency = (parents[..., :, None] == position[None, :]) | (
        position[:, None] == position[None, :]
    )
    closure = adjacency.astype(jnp.float32)
    for doubling in range(max(1, (tree_size - 1).bit_length())):
        closure = jnp.minimum(
            jnp.einsum("...ij,...jk->...ik", closure, closure, precision=lax.Precision.HIGHEST), 1.0
        )
    return closure > 0.5


def tree_attention(queries, cache_keys, cache_values, new_keys, new_values, lengths, allowed):
    scaling = 1.0 / math.sqrt(queries.shape[-1])
    cache_scores = (
        jnp.einsum("rtkgd,rckd->rkgtc", queries, cache_keys, preferred_element_type=jnp.float32)
        * scaling
    )
    tree_scores = (
        jnp.einsum("rtkgd,rskd->rkgts", queries, new_keys, preferred_element_type=jnp.float32)
        * scaling
    )
    live = jnp.arange(cache_keys.shape[1], dtype=jnp.int32)[None, :] < lengths[:, None]
    cache_scores = jnp.where(live[:, None, None, None, :], cache_scores, NEGATIVE)
    tree_scores = jnp.where(allowed[:, None, None, :, :], tree_scores, NEGATIVE)
    highest = jnp.maximum(jnp.max(cache_scores, axis=-1), jnp.max(tree_scores, axis=-1))[..., None]
    cache_exp = jnp.exp(cache_scores - highest)
    tree_exp = jnp.exp(tree_scores - highest)
    denominator = (jnp.sum(cache_exp, axis=-1) + jnp.sum(tree_exp, axis=-1))[..., None]
    cache_probs = (cache_exp / denominator).astype(jnp.bfloat16)
    tree_probs = (tree_exp / denominator).astype(jnp.bfloat16)
    mixed = jnp.einsum(
        "rkgtc,rckd->rtkgd", cache_probs, cache_values, preferred_element_type=jnp.float32
    )
    mixed = mixed + jnp.einsum(
        "rkgts,rskd->rtkgd", tree_probs, new_values, preferred_element_type=jnp.float32
    )
    return mixed.astype(jnp.bfloat16).reshape(queries.shape[0], queries.shape[1], -1)


def shards(
    queries,
    new_keys,
    new_values,
    key_pages,
    value_pages,
    page_table,
    cache_lengths,
    parents,
    residual,
    out_weight,
    norm_gain,
    router_weight,
    routes,
    expert_gate_up,
    expert_down,
    shared_gate_up,
    shared_down,
):
    groups = lax.axis_size("req")
    tp_count = lax.axis_size("tp")
    requests = parents.shape[0]
    tree_size = parents.shape[1]
    row_count = requests * tree_size
    kv_local = new_keys.shape[1] // HD
    head_ratio = QH // KVH
    model_width = residual.shape[1]
    part_width = model_width // tp_count
    pages_dev = key_pages.shape[0]
    local_pages = page_table - lax.axis_index("req") * pages_dev
    cache_keys = key_pages[local_pages].reshape(requests, -1, kv_local, HD)
    cache_values = value_pages[local_pages].reshape(requests, -1, kv_local, HD)
    head_outputs = tree_attention(
        queries.reshape(requests, tree_size, kv_local, head_ratio, HD),
        cache_keys,
        cache_values,
        new_keys.reshape(requests, tree_size, kv_local, HD),
        new_values.reshape(requests, tree_size, kv_local, HD),
        cache_lengths,
        ancestors(parents),
    )
    attn_terms = jnp.dot(
        head_outputs.reshape(row_count, -1), out_weight, preferred_element_type=jnp.float32
    )
    column = lax.axis_index("tp") * part_width
    experts_local = expert_gate_up.shape[0]
    top_count = routes.shape[1]
    expert_count = experts_local * groups
    capacity = max(10 * requests, row_count * top_count * 5 // (4 * expert_count) + 1)
    capacity = -(-capacity // 16) * 16
    slot_count = expert_count * capacity
    flat_expert = routes.reshape(-1)
    expert_ids = jnp.arange(expert_count, dtype=jnp.int32)
    onehot = (flat_expert[:, None] == expert_ids[None, :]).astype(jnp.int32)
    earlier = jnp.cumsum(onehot, axis=0) - onehot
    rank = jnp.sum(earlier * onehot, axis=1)
    slot = (flat_expert * capacity + rank).reshape(row_count, top_count)
    slot_ids = jnp.arange(slot_count, dtype=jnp.int32)
    hit = slot[:, :, None] == slot_ids[None, None, :]
    attn_blocks = attn_terms.astype(jnp.bfloat16).reshape(row_count, tp_count, part_width)
    attn_blocks = lax.all_to_all(
        attn_blocks.transpose(1, 0, 2), "tp", split_axis=0, concat_axis=0, tiled=True
    )
    attn_part = jnp.sum(attn_blocks.astype(jnp.float32), axis=0)
    residual_part = lax.dynamic_slice_in_dim(residual, column, part_width, 1)
    hidden_part_bf = (residual_part.astype(jnp.float32) + attn_part).astype(jnp.bfloat16)
    hidden_bf = lax.all_gather(hidden_part_bf[None], "tp", axis=0, tiled=True)
    hidden = hidden_bf.transpose(1, 0, 2).reshape(row_count, model_width).astype(jnp.float32)
    rstd = lax.rsqrt(jnp.mean(hidden * hidden, axis=1, keepdims=True) + EPSILON)
    normed = hidden * rstd * norm_gain
    logits = jnp.dot(normed, router_weight, precision=lax.Precision.HIGHEST)
    normed_bf = normed.astype(jnp.bfloat16)
    hidden_part = hidden_part_bf.astype(jnp.float32)
    near_width = part_width // 2
    far_width = part_width - near_width
    normed_blocks = normed_bf.reshape(row_count, tp_count, part_width)
    normed_near = normed_blocks[:, :, :near_width].reshape(row_count, tp_count * near_width)
    normed_far = lax.dynamic_slice_in_dim(normed_bf, column + near_width, far_width, 1)
    send_rows = jnp.concatenate([normed_near, normed_far], axis=1)
    dispatch = jnp.any(hit, axis=1).astype(jnp.bfloat16)
    dispatch = dispatch.reshape(row_count, groups, experts_local, capacity)
    returns = []
    for expert in range(experts_local):
        outbox = jnp.einsum(
            "tgc,tk->gck", dispatch[:, :, expert], send_rows, preferred_element_type=jnp.float32
        ).astype(jnp.bfloat16)
        arrived = lax.all_to_all(outbox, "req", split_axis=0, concat_axis=0, tiled=True)
        arrived = arrived.reshape(groups * capacity, -1)
        rows_near = arrived[:, : tp_count * near_width]
        rows_far = lax.all_gather(
            arrived[None, :, tp_count * near_width :], "tp", axis=0, tiled=True
        )
        weight_blocks = expert_gate_up[expert].reshape(tp_count, part_width, 2, -1)
        weight_near = weight_blocks[:, :near_width].reshape(tp_count * near_width, 2, -1)
        weight_far = weight_blocks[:, near_width:]
        gate_up = jnp.einsum(
            "mk,kcf->mcf", rows_near, weight_near, preferred_element_type=jnp.float32
        ) + jnp.einsum("zmk,zkcf->mcf", rows_far, weight_far, preferred_element_type=jnp.float32)
        act = (jax.nn.silu(gate_up[:, 0]) * gate_up[:, 1]).astype(jnp.bfloat16)
        partial_value = jnp.dot(act, expert_down[expert], preferred_element_type=jnp.float32)
        partial_blocks = partial_value.astype(jnp.bfloat16).reshape(-1, tp_count, part_width)
        back_near = partial_blocks[:, :, :near_width].reshape(-1, tp_count * near_width)
        far_parts = lax.all_to_all(
            partial_blocks[:, :, near_width:].transpose(1, 0, 2),
            "tp",
            split_axis=0,
            concat_axis=0,
            tiled=True,
        )
        back_far = jnp.sum(far_parts.astype(jnp.float32), axis=0).astype(jnp.bfloat16)
        outputs = jnp.concatenate([back_near, back_far], axis=1).reshape(groups, capacity, -1)
        returns.append(lax.all_to_all(outputs, "req", split_axis=0, concat_axis=0, tiled=True))
    chosen = jnp.sum(
        jnp.where(routes[:, :, None] == expert_ids[None, None, :], logits[:, None, :], 0.0), axis=-1
    )
    gate_values = jax.nn.sigmoid(chosen)
    gate_values = gate_values / jnp.sum(gate_values, axis=1, keepdims=True)
    weights = jnp.sum(jnp.where(hit, gate_values[:, :, None], 0.0), axis=1)
    weights = weights.reshape(row_count, groups, experts_local, capacity)
    weights_hi = weights.astype(jnp.bfloat16)
    weights_lo = (weights - weights_hi.astype(jnp.float32)).astype(jnp.bfloat16)
    routed = jnp.zeros((row_count, tp_count * near_width + far_width), jnp.float32)
    for expert in range(experts_local):
        for split in (weights_hi, weights_lo):
            routed = routed + jnp.einsum(
                "tgc,gck->tk",
                split[:, :, expert],
                returns[expert],
                preferred_element_type=jnp.float32,
            )
    routed_near = routed[:, : tp_count * near_width].reshape(row_count, tp_count, near_width)
    routed_far = routed[:, tp_count * near_width :]
    shared_gu = jnp.einsum(
        "td,dcf->tcf", normed_bf, shared_gate_up, preferred_element_type=jnp.float32
    )
    shared_act = (jax.nn.silu(shared_gu[:, 0]) * shared_gu[:, 1]).astype(jnp.bfloat16)
    shared_terms = jnp.dot(shared_act, shared_down, preferred_element_type=jnp.float32)
    shared_blocks = shared_terms.reshape(row_count, tp_count, part_width)
    total = jnp.concatenate(
        [shared_blocks[:, :, :near_width] + routed_near, shared_blocks[:, :, near_width:]], axis=2
    ).astype(jnp.bfloat16)
    total = lax.all_to_all(total.transpose(1, 0, 2), "tp", split_axis=0, concat_axis=0, tiled=True)
    summed = jnp.sum(total.astype(jnp.float32), axis=0)
    summed = summed + jnp.concatenate(
        [jnp.zeros((row_count, near_width), jnp.float32), routed_far], axis=1
    )
    return (hidden_part + summed).astype(jnp.bfloat16)


def solution(mesh):
    in_specs = (
        P("req", "tp"),
        P("req", "tp"),
        P("req", "tp"),
        P("req", None, "tp"),
        P("req", None, "tp"),
        P("req", None),
        P("req"),
        P("req", None),
        P("req", None),
        P("tp", None),
        P(),
        P(),
        P("req", None),
        P("req", None, None, "tp"),
        P("req", "tp", None),
        P(None, None, "tp"),
        P("tp", None),
    )
    out_specs = P("req", "tp")
    return jax.shard_map(shards, mesh=mesh, in_specs=in_specs, out_specs=out_specs, check_vma=False)
```

profile of v0, /device:TPU:2, one launch (start us, length us, event | category | flops | bytes accessed | tf_op | source)
XLA Modules:
  0.0 446.8 jit_solution(14865229061335307913)
XLA Ops:
  28.5 4.9 %all-to-all-start = ((bf16[4,192,640]{2,1,0:T(8,128)(2,1)}), bf16[4,192,640]{2,1,0:T(8,128)(2,1)S(1)}, u32[]{:S(2)}, u32[]{:S(2)}) async-start(bf16[4,192,640]{2,1,0:T(8,128)(2,1)} %bitcast.226), calls=%async_computation | async-start | bytes 1966080 | tf_op jit(solution)/shard_map/all_to_all | solution.py:120
  41.8 15.9 %all-to-all-done = bf16[4,192,640]{2,1,0:T(8,128)(2,1)S(1)} async-done(((bf16[4,192,640]{2,1,0:T(8,128)(2,1)}), bf16[4,192,640]{2,1,0:T(8,128)(2,1)S(1)}, u32[]{:S(2)}, u32[]{:S(2)}) %all-to-all-start) | async-done | bytes 983072 | tf_op jit(solution)/shard_map/all_to_all | solution.py:120
  58.8 19.7 %all-gather = bf16[768,640]{1,0:T(8,128)(2,1)S(1)} all-gather(bf16[192,640]{1,0:T(8,128)(2,1)S(1)} %add_convert_fusion.1), channel_id=2, replica_groups=mesh['req'=8,'tp'=4] {'tp'}, dimensions={0}, use_global_device_ids=true | all-gather | bytes 1228800 | tf_op jit(solution)/shard_map/all_gather | solution.py:126
  86.8 34.1 %all_to_all.40 = bf16[8,96,1600]{2,1,0:T(8,128)(2,1)S(1)} all-to-all(bf16[8,96,1600]{2,1,0:T(8,128)(2,1)S(1)} %convolution_convert_fusion.4), channel_id=1, replica_groups=mesh['req'=8,'tp'=4] {'req'}, dimensions={0} | all-to-all | bytes 4915200 | tf_op jit(solution)/shard_map/all_to_all | solution.py:146
  125.7 5.7 %all-to-all-start.4 = ((bf16[8,96,1600]{2,1,0:T(8,128)(2,1)}), bf16[8,96,1600]{2,1,0:T(8,128)(2,1)}, u32[]{:S(2)}, u32[]{:S(2)}) async-start(bf16[8,96,1600]{2,1,0:T(8,128)(2,1)} %convolution_convert_fusion.3), calls=%async_computation.4 | async-start | bytes 5111808 | tf_op jit(solution)/shard_map/all_to_all | solution.py:146
  131.7 7.6 %fusion.67 = (bf16[1,2560,2,384]{3,2,1,0:T(2,128)(2,1)S(1)}, bf16[1,2560,2,384]{3,2,1,0:T(2,128)(2,1)}) fusion(bf16[2,2560,2,384]{3,2,1,0:T(2,128)(2,1)} %param.30), kind=kLoop, calls=%fused_computation.137 | loop fusion | bytes 15728640 | tf_op jit(solution)/shard_map/slice | solution.py:152
  143.2 18.4 %all-to-all-done.4 = bf16[8,96,1600]{2,1,0:T(8,128)(2,1)} async-done(((bf16[8,96,1600]{2,1,0:T(8,128)(2,1)}), bf16[8,96,1600]{2,1,0:T(8,128)(2,1)}, u32[]{:S(2)}, u32[]{:S(2)}) %all-to-all-start.4) | async-done | bytes 2457632 | tf_op jit(solution)/shard_map/all_to_all | solution.py:146
  163.6 9.5 %all-gather.6.cloned.1.call-done = bf16[3072,320]{1,0:T(8,128)(2,1)} async-done(((bf16[768,320]{1,0:T(8,128)(2,1)}), bf16[3072,320]{1,0:T(8,128)(2,1)}) %all-gather.6.cloned.1.call-update) | async-done | bytes 1966096 | tf_op jit(solution)/shard_map/all_gather | solution.py:149
  183.7 7.6 %reshape.244 = bf16[768,4,640]{2,1,0:T(4,128)(2,1)} reshape(bf16[768,2560]{1,0:T(8,128)(2,1)} %convolution_convert_fusion.1) | data formatting | bytes 7864320 | tf_op jit(solution)/shard_map/reshape | solution.py:160
  191.3 7.4 %fusion.68 = (bf16[768,4,320]{2,1,0:T(4,128)(2,1)}, bf16[768,4,320]{2,1,0:T(4,128)(2,1)}) fusion(bf16[768,4,640]{2,1,0:T(4,128)(2,1)} %reshape.244), kind=kLoop, calls=%fused_computation.138 | loop fusion | bytes 7864320 | tf_op jit(solution)/shard_map/slice | solution.py:161
  198.7 5.4 %copy.182 = bf16[768,4,320]{0,2,1:T(8,128)(2,1)} copy(bf16[768,4,320]{2,1,0:T(4,128)(2,1)} %get-tuple-element.8) | data formatting | bytes 3932160
  204.0 4.8 %all-to-all-start.2 = ((bf16[4,768,320]{1,2,0:T(8,128)(2,1)}), bf16[4,768,320]{1,2,0:T(8,128)(2,1)}, u32[]{:S(2)}, u32[]{:S(2)}) async-start(bf16[4,768,320]{1,2,0:T(8,128)(2,1)} %bitcast.238), calls=%async_computation.2 | async-start | bytes 3932160 | tf_op jit(solution)/shard_map/all_to_all | solution.py:162
  214.9 25.5 %all-gather.8.cloned.1.call-done = bf16[3072,320]{1,0:T(8,128)(2,1)} async-done(((bf16[768,320]{1,0:T(8,128)(2,1)}), bf16[3072,320]{1,0:T(8,128)(2,1)}) %all-gather.8.cloned.1.call-update) | async-done | bytes 1966096 | tf_op jit(solution)/shard_map/all_gather | solution.py:149
  252.1 7.6 %reshape.247 = bf16[768,4,640]{2,1,0:T(4,128)(2,1)} reshape(bf16[768,2560]{1,0:T(8,128)(2,1)} %convolution_convert_fusion) | data formatting | bytes 7864320 | tf_op jit(solution)/shard_map/reshape | solution.py:160
  259.7 7.3 %fusion.69 = (bf16[768,4,320]{2,1,0:T(4,128)(2,1)}, bf16[768,4,320]{2,1,0:T(4,128)(2,1)}) fusion(bf16[768,4,640]{2,1,0:T(4,128)(2,1)} %reshape.247), kind=kLoop, calls=%fused_computation.139 | loop fusion | bytes 7864320 | tf_op jit(solution)/shard_map/slice | solution.py:161
  267.0 5.3 %copy.184 = bf16[768,4,320]{0,2,1:T(8,128)(2,1)} copy(bf16[768,4,320]{2,1,0:T(4,128)(2,1)} %get-tuple-element.10) | data formatting | bytes 3932160
  276.8 4.7 %concatenate.27 = bf16[8,96,1280]{2,1,0:T(8,128)(2,1)} reshape(bf16[768,4,320]{2,1,0:T(4,128)(2,1)} %get-tuple-element.7) | data formatting | bytes 3932160 | tf_op jit(solution)/shard_map/concatenate | solution.py:170
  287.1 34.9 %all-to-all-done.5 = bf16[4,768,320]{1,2,0:T(8,128)(2,1)} async-done(((bf16[4,768,320]{1,2,0:T(8,128)(2,1)}), bf16[4,768,320]{1,2,0:T(8,128)(2,1)}, u32[]{:S(2)}, u32[]{:S(2)}) %all-to-all-start.5) | async-done | bytes 1966112 | tf_op jit(solution)/shard_map/all_to_all | solution.py:162
  322.0 4.8 %all-to-all-start.3 = ((bf16[8,96,1600]{2,1,0:T(8,128)(2,1)}), bf16[8,96,1600]{2,1,0:T(8,128)(2,1)}, u32[]{:S(2)}, u32[]{:S(2)}) async-start(bf16[8,96,1600]{2,1,0:T(8,128)(2,1)} %pad_maximum_fusion), calls=%async_computation.3 | async-start | bytes 5111808 | tf_op jit(solution)/shard_map/all_to_all | solution.py:171
  330.9 4.7 %concatenate.30 = bf16[8,96,1280]{2,1,0:T(8,128)(2,1)} reshape(bf16[768,4,320]{2,1,0:T(4,128)(2,1)} %get-tuple-element.9) | data formatting | bytes 3932160 | tf_op jit(solution)/shard_map/concatenate | solution.py:170
  341.2 15.8 %all-to-all-done.3 = bf16[8,96,1600]{2,1,0:T(8,128)(2,1)} async-done(((bf16[8,96,1600]{2,1,0:T(8,128)(2,1)}), bf16[8,96,1600]{2,1,0:T(8,128)(2,1)}, u32[]{:S(2)}, u32[]{:S(2)}) %all-to-all-start.3) | async-done | bytes 2457632 | tf_op jit(solution)/shard_map/all_to_all | solution.py:171
  357.0 6.0 %all-to-all-start.6 = ((bf16[8,96,1600]{2,1,0:T(8,128)(2,1)}), bf16[8,96,1600]{2,1,0:T(8,128)(2,1)}, u32[]{:S(2)}, u32[]{:S(2)}) async-start(bf16[8,96,1600]{2,1,0:T(8,128)(2,1)} %pad_maximum_fusion.1), calls=%async_computation.6 | async-start | bytes 5111808 | tf_op jit(solution)/shard_map/all_to_all | solution.py:171
  377.9 15.3 %all-to-all-done.6 = bf16[8,96,1600]{2,1,0:T(8,128)(2,1)} async-done(((bf16[8,96,1600]{2,1,0:T(8,128)(2,1)}), bf16[8,96,1600]{2,1,0:T(8,128)(2,1)}, u32[]{:S(2)}, u32[]{:S(2)}) %all-to-all-start.6) | async-done | bytes 2457632 | tf_op jit(solution)/shard_map/all_to_all | solution.py:171
  413.4 23.2 %all-to-all-done.7 = bf16[4,192,640]{2,1,0:T(8,128)(2,1)} async-done(((bf16[4,192,640]{2,1,0:T(8,128)(2,1)}), bf16[4,192,640]{2,1,0:T(8,128)(2,1)}, u32[]{:S(2)}, u32[]{:S(2)}) %all-to-all-start.7) | async-done | bytes 983072 | tf_op jit(solution)/shard_map/all_to_all | solution.py:201
  (157 shorter events, 136.3 us)
Async XLA Ops:
  6.5 19.9 %copy-start = (bf16[640,2560]{1,0:T(8,128)(2,1)S(1)}, bf16[640,2560]{1,0:T(8,128)(2,1)}, u32[]{:S(2)}) copy-start(bf16[640,2560]{1,0:T(8,128)(2,1)} %param.26) | copy-start | bytes 9830404
  15.4 2.2 copy-start.23
  22.5 3.5 copy-start.14
  22.5 3.5 copy-start.26
  27.4 5.9 %copy-start.22 = (s32[192,6]{0,1:T(8,128)S(1)}, s32[192,6]{0,1:T(8,128)}, u32[]{:S(2)}) copy-start(s32[192,6]{0,1:T(8,128)} %param.29) | copy-start | bytes 13828
  27.4 6.3 %copy-start.21 = (f32[2560]{0:T(1024)S(1)}, f32[2560]{0:T(1024)}, u32[]{:S(2)}) copy-start(f32[2560]{0:T(1024)} %param.27) | copy-start | bytes 30724
  28.5 29.2 %all-to-all-start = ((bf16[4,192,640]{2,1,0:T(8,128)(2,1)}), bf16[4,192,640]{2,1,0:T(8,128)(2,1)S(1)}, u32[]{:S(2)}, u32[]{:S(2)}) async-start(bf16[4,192,640]{2,1,0:T(8,128)(2,1)} %bitcast.226), calls=%async_computation | async-start | bytes 1966080 | tf_op jit(solution)/shard_map/all_to_all | solution.py:120
  33.4 139.8 %all-gather.6.cloned.1.call-start = ((), (), s32[]{:S(2)}) async-start(), calls=%async_computation.8 | async-start | bytes 2949120 | tf_op jit(solution)/shard_map/all_gather | solution.py:149
  125.7 35.9 %all-to-all-start.4 = ((bf16[8,96,1600]{2,1,0:T(8,128)(2,1)}), bf16[8,96,1600]{2,1,0:T(8,128)(2,1)}, u32[]{:S(2)}, u32[]{:S(2)}) async-start(bf16[8,96,1600]{2,1,0:T(8,128)(2,1)} %convolution_convert_fusion.3), calls=%async_computation.4 | async-start | bytes 5111808 | tf_op jit(solution)/shard_map/all_to_all | solution.py:146
  131.5 108.9 %all-gather.8.cloned.1.call-start = ((), (), s32[]{:S(2)}) async-start(), calls=%async_computation.9 | async-start | bytes 2949120 | tf_op jit(solution)/shard_map/all_gather | solution.py:149
  173.2 4.2 copy-start.10
  173.2 4.2 copy-start.15
  204.0 68.3 %all-to-all-start.2 = ((bf16[4,768,320]{1,2,0:T(8,128)(2,1)}), bf16[4,768,320]{1,2,0:T(8,128)(2,1)}, u32[]{:S(2)}, u32[]{:S(2)}) async-start(bf16[4,768,320]{1,2,0:T(8,128)(2,1)} %bitcast.238), calls=%async_computation.2 | async-start | bytes 3932160 | tf_op jit(solution)/shard_map/all_to_all | solution.py:162
  240.4 4.1 copy-start.16
  244.5 3.5 copy-start.25
  272.3 49.7 %all-to-all-start.5 = ((bf16[4,768,320]{1,2,0:T(8,128)(2,1)}), bf16[4,768,320]{1,2,0:T(8,128)(2,1)}, u32[]{:S(2)}, u32[]{:S(2)}) async-start(bf16[4,768,320]{1,2,0:T(8,128)(2,1)} %bitcast.239), calls=%async_computation.5 | async-start | bytes 3932160 | tf_op jit(solution)/shard_map/all_to_all | solution.py:162
  322.0 35.0 %all-to-all-start.3 = ((bf16[8,96,1600]{2,1,0:T(8,128)(2,1)}), bf16[8,96,1600]{2,1,0:T(8,128)(2,1)}, u32[]{:S(2)}, u32[]{:S(2)}) async-start(bf16[8,96,1600]{2,1,0:T(8,128)(2,1)} %pad_maximum_fusion), calls=%async_computation.3 | async-start | bytes 5111808 | tf_op jit(solution)/shard_map/all_to_all | solution.py:171
  341.2 21.8 %copy-start.20 = (f32[2560,16]{0,1:T(8,128)S(1)}, f32[2560,16]{0,1:T(8,128)}, u32[]{:S(2)}) copy-start(f32[2560,16]{0,1:T(8,128)} %param.28) | copy-start | bytes 491524
  357.0 36.2 %all-to-all-start.6 = ((bf16[8,96,1600]{2,1,0:T(8,128)(2,1)}), bf16[8,96,1600]{2,1,0:T(8,128)(2,1)}, u32[]{:S(2)}, u32[]{:S(2)}) async-start(bf16[8,96,1600]{2,1,0:T(8,128)(2,1)} %pad_maximum_fusion.1), calls=%async_computation.6 | async-start | bytes 5111808 | tf_op jit(solution)/shard_map/all_to_all | solution.py:171
  368.9 26.7 %copy-start.17 = (bf16[192,8,2,96]{3,0,1,2:T(8,128)(2,1)}, bf16[192,8,2,96]{3,0,1,2:T(8,128)(2,1)S(1)}, u32[]{:S(2)}) copy-start(bf16[192,8,2,96]{3,0,1,2:T(8,128)(2,1)S(1)} %copy.207) | copy-start | bytes 1769476
  368.9 3.7 copy-start.5
  401.9 3.1 copy-start.7
  406.0 33.8 %copy-start.1 = (bf16[640,2560]{1,0:T(8,128)(2,1)S(1)}, bf16[640,2560]{1,0:T(8,128)(2,1)}, u32[]{:S(2)}) copy-start(bf16[640,2560]{1,0:T(8,128)(2,1)} %param.26) | copy-start | bytes 9830404
  407.4 29.3 %all-to-all-start.7 = ((bf16[4,192,640]{2,1,0:T(8,128)(2,1)}), bf16[4,192,640]{2,1,0:T(8,128)(2,1)}, u32[]{:S(2)}, u32[]{:S(2)}) async-start(bf16[4,192,640]{2,1,0:T(8,128)(2,1)} %maximum_bitcast_fusion), calls=%async_computation.7 | async-start | bytes 1966080 | tf_op jit(solution)/shard_map/all_to_all | solution.py:201
  (12 other events, 19.2 us)
Sparse Core Ops, SparseCore 0:
  123.5 49.6 all-gather.5
  174.7 65.5 all-gather.7
where the time goes:
time: 455 us; the launch traced here: 447 us
  waiting for transfers between devices  158 us (35%)
  local copies, waits for them, and re-layouts  105 us (23%)
  blocking collectives  53.8 us (12%)
  matrix products  50.7 us (11%)
  starting transfers between devices  35.3 us (8%)
  other arithmetic  28.9 us (6%)
  between operations  14.3 us (3%)
    all_gather x2, waiting for transfers between devices, shards(): lax.all_gather(arrived[None, :, tp_count * near_width:], 'tp', axis=0, ti...  35 us
    all_to_all x2, waiting for transfers between devices, shards(): lax.all_to_all(partial_blocks[:, :, near_width:].transpose(1, 0, 2), 'tp'...  34.9 us
    all_to_all x1, blocking collectives, shards(): lax.all_to_all(outbox, 'req', split_axis=0, concat_axis=0, tiled=True)  34.1 us
    all_to_all x2, waiting for transfers between devices, shards(): lax.all_to_all(outputs, 'req', split_axis=0, concat_axis=0, tiled=True)  31 us
    all_to_all x1, waiting for transfers between devices, shards(): lax.all_to_all(total.transpose(1, 0, 2), 'tp', split_axis=0, concat_axis=...  23.2 us
    unnamed x58, local copies, waits for them, and re-layouts  21.6 us
    all_gather x1, blocking collectives, shards(): hidden_bf = lax.all_gather(hidden_part_bf[None], 'tp', axis=0, tiled=True)  19.7 us
    all_to_all x1, waiting for transfers between devices, shards(): lax.all_to_all(outbox, 'req', split_axis=0, concat_axis=0, tiled=True)  18.4 us
  transfers between devices with their start and end apart: 9, of which 8 were waited for; matrix products, arithmetic and copies ran while one was open for 29% of the time, Pallas kernels for 0%

commit v1 on v0

--- a/solution.py
+++ b/solution.py
@@ -9,6 +9,18 @@
 HD = 128
 EPSILON = 1e-06
 NEGATIVE = -1e30
+
+
+def doubled_up(shard, axis, dim):
+    ways, here = (lax.axis_size(axis), lax.axis_index(axis))
+    grown, reach = (shard, 1)
+    while reach < ways:
+        theirs = lax.ppermute(grown, axis, [(d, d ^ reach) for d in range(ways)])
+        mine_first = jnp.concatenate([grown, theirs], axis=dim)
+        theirs_first = jnp.concatenate([theirs, grown], axis=dim)
+        grown = jnp.where(here & reach == 0, mine_first, theirs_first)
+        reach = 2 * reach
+    return grown
 
 
 def rounded(values):
@@ -146,9 +158,7 @@
         arrived = lax.all_to_all(outbox, "req", split_axis=0, concat_axis=0, tiled=True)
         arrived = arrived.reshape(groups * capacity, -1)
         rows_near = arrived[:, : tp_count * near_width]
-        rows_far = lax.all_gather(
-            arrived[None, :, tp_count * near_width :], "tp", axis=0, tiled=True
-        )
+        rows_far = doubled_up(arrived[None, :, tp_count * near_width :], "tp", 0)
         weight_blocks = expert_gate_up[expert].reshape(tp_count, part_width, 2, -1)
         weight_near = weight_blocks[:, :near_width].reshape(tp_count * near_width, 2, -1)
         weight_far = weight_blocks[:, near_width:]

time: 455 us -> 516 us (1.13)
  waiting for transfers between devices: 158 us -> 235 us
  blocking collectives: 53.8 us -> 19.7 us
  between operations: 14.3 us -> 0.83 us
  matrix products: 50.7 us -> 62.6 us
  starting transfers between devices: 35.3 us -> 47.1 us
    ppermute x0 -> x4, waiting for transfers between devices: none -> 108 us  [doubled_up(): theirs = lax.ppermute(grown, axis, [(d, d ^ reach) for d in range(ways)])]
    all_gather x2 -> x0, waiting for transfers between devices: 35 us -> none  [shards(): lax.all_gather(arrived[None, :, tp_count * near_width:], 'tp', axis=0, ti...]
    all_to_all x1 -> x0, blocking collectives: 34.1 us -> none  [shards(): lax.all_to_all(outbox, 'req', split_axis=0, concat_axis=0, tiled=True)]
    all_to_all x1 -> x2, waiting for transfers between devices: 18.4 us -> 27.8 us  [shards(): lax.all_to_all(outbox, 'req', split_axis=0, concat_axis=0, tiled=True)]
    ppermute x0 -> x4, local copies, waits for them, and re-layouts: none -> 7.42 us  [doubled_up(): theirs = lax.ppermute(grown, axis, [(d, d ^ reach) for d in range(ways)])]
    unnamed x58, local copies, waits for them, and re-layouts: 21.6 us -> 15 us
    ppermute x0 -> x4, starting transfers between devices: none -> 6.43 us  [doubled_up(): theirs = lax.ppermute(grown, axis, [(d, d ^ reach) for d in range(ways)])]
    all_to_all x2, waiting for transfers between devices: 31 us -> 24.7 us  [shards(): lax.all_to_all(outputs, 'req', split_axis=0, concat_axis=0, tiled=True)]
  transfers between devices with their start and end apart: 9 -> 12, of which waited for: 8 -> 9; matrix products, arithmetic and copies ran while one was open for 29% -> 31% of each run, Pallas kernels for 0% -> 0%
where the time goes in v1:
time: 516 us; the launch traced here: 507 us
  waiting for transfers between devices  235 us (46%)
  local copies, waits for them, and re-layouts  110 us (21%)
  matrix products  62.6 us (12%)
  starting transfers between devices  47.1 us (9%)
  other arithmetic  32.7 us (6%)
  blocking collectives  19.7 us (4%)
    ppermute x4, waiting for transfers between devices, doubled_up(): theirs = lax.ppermute(grown, axis, [(d, d ^ reach) for d in range(ways)])  108 us
    all_to_all x2, waiting for transfers between devices, shards(): lax.all_to_all(partial_blocks[:, :, near_width:].transpose(1, 0, 2), 'tp'...  34.7 us
    all_to_all x2, waiting for transfers between devices, shards(): lax.all_to_all(outbox, 'req', split_axis=0, concat_axis=0, tiled=True)  27.8 us
    all_to_all x2, waiting for transfers between devices, shards(): lax.all_to_all(outputs, 'req', split_axis=0, concat_axis=0, tiled=True)  24.7 us
    all_to_all x1, waiting for transfers between devices, shards(): lax.all_to_all(total.transpose(1, 0, 2), 'tp', split_axis=0, concat_axis=...  23.2 us
    all_gather x1, blocking collectives, shards(): hidden_bf = lax.all_gather(hidden_part_bf[None], 'tp', axis=0, tiled=True)  19.7 us
    all_to_all x1, waiting for transfers between devices, shards(): lax.all_to_all(attn_blocks.transpose(1, 0, 2), 'tp', split_axis=0, concat...  15.9 us
    reshape x2, local copies, waits for them, and re-layouts, shards(): partial_value.astype(jnp.bfloat16).reshape(-1, tp_count, part_width)  15.2 us
  transfers between devices with their start and end apart: 12, of which 9 were waited for; matrix products, arithmetic and copies ran while one was open for 31% of the time, Pallas kernels for 0%

profile of v1, /device:TPU:2, one launch (start us, length us, event | category | flops | bytes accessed | tf_op | source)
XLA Modules:
  0.0 507.5 jit_solution(17513931402715952241)
XLA Ops:
  31.1 15.9 %all-to-all-done = bf16[4,192,640]{2,1,0:T(8,128)(2,1)S(1)} async-done(((bf16[4,192,640]{2,1,0:T(8,128)(2,1)}), bf16[4,192,640]{2,1,0:T(8,128)(2,1)S(1)}, u32[]{:S(2)}, u32[]{:S(2)}) %all-to-all-start) | async-done | bytes 983072 | tf_op jit(solution)/shard_map/all_to_all | solution.py:132
  48.2 19.7 %all-gather = bf16[768,640]{1,0:T(8,128)(2,1)S(1)} all-gather(bf16[192,640]{1,0:T(8,128)(2,1)S(1)} %add_convert_fusion.1), channel_id=2, replica_groups=mesh['req'=8,'tp'=4] {'tp'}, dimensions={0}, use_global_device_ids=true | all-gather | bytes 1228800 | tf_op jit(solution)/shard_map/all_gather | solution.py:138
  85.9 27.8 %all-to-all-done.4 = bf16[8,96,1600]{2,1,0:T(8,128)(2,1)} async-done(((bf16[8,96,1600]{2,1,0:T(8,128)(2,1)}), bf16[8,96,1600]{2,1,0:T(8,128)(2,1)}, u32[]{:S(2)}, u32[]{:S(2)}) %all-to-all-start.4) | async-done | bytes 2457632 | tf_op jit(solution)/shard_map/all_to_all | solution.py:158
  113.7 6.1 %all-to-all-start.1 = ((bf16[8,96,1600]{2,1,0:T(8,128)(2,1)}), bf16[8,96,1600]{2,1,0:T(8,128)(2,1)}, u32[]{:S(2)}, u32[]{:S(2)}) async-start(bf16[8,96,1600]{2,1,0:T(8,128)(2,1)} %convolution_convert_fusion.4), calls=%async_computation.1 | async-start | bytes 5111808 | tf_op jit(solution)/shard_map/all_to_all | solution.py:158
  121.6 13.0 %collective-permute-done.2 = bf16[1,768,320]{1,2,0:T(8,128)(2,1)} collective-permute-done((bf16[1,768,320]{1,2,0:T(8,128)(2,1)S(1)}, bf16[1,768,320]{1,2,0:T(8,128)(2,1)}, u32[]{:S(2)}, u32[]{:S(2)}) %collective-permute-start.2) | collective-permute-done | bytes 491552 | tf_op jit(solution)/shard_map/ppermute | solution.py:18
  140.9 7.6 %fusion.93 = (bf16[1,2560,2,384]{3,2,1,0:T(2,128)(2,1)}, bf16[1,2560,2,384]{3,2,1,0:T(2,128)(2,1)S(1)}) fusion(bf16[2,2560,2,384]{3,2,1,0:T(2,128)(2,1)} %param.30), kind=kLoop, calls=%fused_computation.159 | loop fusion | bytes 15728640 | tf_op jit(solution)/shard_map/slice | solution.py:162
  155.6 5.2 %fusion.27 = f32[768,2,384]{2,0,1:T(8,128)} fusion(bf16[1280,2,384]{2,0,1:T(8,128)(2,1)} %bitcast.248, bf16[768,1600]{1,0:T(8,128)(2,1)} %bitcast.53), kind=kOutput, calls=%fused_computation.49 | convolution fusion | flops 1509949440 | bytes 6291456 | tf_op jit(solution)/shard_map/mk,kcf->mcf/dot_general | solution.py:165
  160.8 24.0 %collective-permute-done.3 = bf16[2,768,320]{1,2,0:T(8,128)(2,1)} collective-permute-done((bf16[2,768,320]{1,2,0:T(8,128)(2,1)}, bf16[2,768,320]{1,2,0:T(8,128)(2,1)}, u32[]{:S(2)}, u32[]{:S(2)}) %collective-permute-start.3) | collective-permute-done | bytes 983072 | tf_op jit(solution)/shard_map/ppermute | solution.py:18
  187.3 5.8 %bitcast_add_fusion = f32[768,2,384]{2,0,1:T(8,128)S(1)} fusion(f32[768,2,384]{2,0,1:T(8,128)} %fusion.27, bf16[4,640,2,384]{3,1,0,2:T(8,128)(2,1)} %bitcast.236, bf16[2,768,320]{2,1,0:T(8,128)(2,1)} %copy.211, bf16[2,768,320]{2,1,0:T(8,128)(2,1)} %maximum_select_fusion.3, pred[]{:T(512)S(6)} %eq.109), kind=kOutput, calls=%fused_computation.43 | convolution fusion | flops 1519386624 | bytes 9043969 | tf_op jit(solution)/shard_map/zmk,zkcf->mcf/dot_general | solution.py:167
  197.3 7.6 %reshape.247 = bf16[768,4,640]{2,1,0:T(4,128)(2,1)} reshape(bf16[768,2560]{1,0:T(8,128)(2,1)} %convolution_convert_fusion) | data formatting | bytes 7864320 | tf_op jit(solution)/shard_map/reshape | solution.py:170
  204.9 7.4 %fusion.95 = (bf16[768,4,320]{2,1,0:T(4,128)(2,1)}, bf16[768,4,320]{2,1,0:T(4,128)(2,1)}) fusion(bf16[768,4,640]{2,1,0:T(4,128)(2,1)} %reshape.247), kind=kLoop, calls=%fused_computation.161 | loop fusion | bytes 7864320 | tf_op jit(solution)/shard_map/slice | solution.py:171
  212.3 5.4 %copy.232 = bf16[768,4,320]{0,2,1:T(8,128)(2,1)} copy(bf16[768,4,320]{2,1,0:T(4,128)(2,1)} %get-tuple-element.10) | data formatting | bytes 3932160
  233.3 5.9 %fusion.29 = f32[768,2,384]{2,0,1:T(8,128)} fusion(bf16[1280,2,384]{2,0,1:T(8,128)(2,1)S(1)} %bitcast.249, bf16[768,1600]{1,0:T(8,128)(2,1)} %bitcast.36), kind=kOutput, calls=%fused_computation.52 | convolution fusion | flops 1509949440 | bytes 6291456 | tf_op jit(solution)/shard_map/mk,kcf->mcf/dot_general | solution.py:165
  239.2 71.3 %collective-permute-done.1 = bf16[2,768,320]{1,2,0:T(8,128)(2,1)} collective-permute-done((bf16[2,768,320]{1,2,0:T(8,128)(2,1)}, bf16[2,768,320]{1,2,0:T(8,128)(2,1)}, u32[]{:S(2)}, u32[]{:S(2)}) %collective-permute-start.1) | collective-permute-done | bytes 983072 | tf_op jit(solution)/shard_map/ppermute | solution.py:18
  312.9 5.1 %bitcast_add_fusion.1 = f32[768,2,384]{2,0,1:T(8,128)S(1)} fusion(f32[768,2,384]{2,0,1:T(8,128)} %fusion.29, bf16[4,640,2,384]{3,1,0,2:T(8,128)(2,1)} %bitcast.238, bf16[2,768,320]{2,1,0:T(8,128)(2,1)} %copy.199, bf16[2,768,320]{2,1,0:T(8,128)(2,1)S(1)} %copy-done.7, pred[]{:T(512)S(6)} %eq.109), kind=kOutput, calls=%fused_computation.44 | convolution fusion | flops 1519386624 | bytes 8847361 | tf_op jit(solution)/shard_map/zmk,zkcf->mcf/dot_general | solution.py:167
  322.1 7.6 %reshape.244 = bf16[768,4,640]{2,1,0:T(4,128)(2,1)} reshape(bf16[768,2560]{1,0:T(8,128)(2,1)} %convolution_convert_fusion.1) | data formatting | bytes 7864320 | tf_op jit(solution)/shard_map/reshape | solution.py:170
  329.7 7.3 %fusion.94 = (bf16[768,4,320]{2,1,0:T(4,128)(2,1)}, bf16[768,4,320]{2,1,0:T(4,128)(2,1)}) fusion(bf16[768,4,640]{2,1,0:T(4,128)(2,1)} %reshape.244), kind=kLoop, calls=%fused_computation.160 | loop fusion | bytes 7864320 | tf_op jit(solution)/shard_map/slice | solution.py:171
  337.0 5.3 %copy.230 = bf16[768,4,320]{0,2,1:T(8,128)(2,1)} copy(bf16[768,4,320]{2,1,0:T(4,128)(2,1)} %get-tuple-element.8) | data formatting | bytes 3932160
  357.1 34.7 %all-to-all-done.2 = bf16[4,768,320]{1,2,0:T(8,128)(2,1)} async-done(((bf16[4,768,320]{1,2,0:T(8,128)(2,1)}), bf16[4,768,320]{1,2,0:T(8,128)(2,1)}, u32[]{:S(2)}, u32[]{:S(2)}) %all-to-all-start.2) | async-done | bytes 1966112 | tf_op jit(solution)/shard_map/all_to_all | solution.py:172
  391.8 5.1 %all-to-all-start.6 = ((bf16[8,96,1600]{2,1,0:T(8,128)(2,1)}), bf16[8,96,1600]{2,1,0:T(8,128)(2,1)}, u32[]{:S(2)}, u32[]{:S(2)}) async-start(bf16[8,96,1600]{2,1,0:T(8,128)(2,1)} %pad_maximum_fusion.1), calls=%async_computation.6 | async-start | bytes 5111808 | tf_op jit(solution)/shard_map/all_to_all | solution.py:181
  415.3 11.8 %all-to-all-done.6 = bf16[8,96,1600]{2,1,0:T(8,128)(2,1)} async-done(((bf16[8,96,1600]{2,1,0:T(8,128)(2,1)}), bf16[8,96,1600]{2,1,0:T(8,128)(2,1)}, u32[]{:S(2)}, u32[]{:S(2)}) %all-to-all-start.6) | async-done | bytes 2457632 | tf_op jit(solution)/shard_map/all_to_all | solution.py:181
  427.1 5.8 %all-to-all-start.3 = ((bf16[8,96,1600]{2,1,0:T(8,128)(2,1)}), bf16[8,96,1600]{2,1,0:T(8,128)(2,1)}, u32[]{:S(2)}, u32[]{:S(2)}) async-start(bf16[8,96,1600]{2,1,0:T(8,128)(2,1)} %pad_maximum_fusion), calls=%async_computation.3 | async-start | bytes 5111808 | tf_op jit(solution)/shard_map/all_to_all | solution.py:181
  450.2 12.9 %all-to-all-done.3 = bf16[8,96,1600]{2,1,0:T(8,128)(2,1)} async-done(((bf16[8,96,1600]{2,1,0:T(8,128)(2,1)}), bf16[8,96,1600]{2,1,0:T(8,128)(2,1)}, u32[]{:S(2)}, u32[]{:S(2)}) %all-to-all-start.3) | async-done | bytes 2457632 | tf_op jit(solution)/shard_map/all_to_all | solution.py:181
  480.9 23.2 %all-to-all-done.7 = bf16[4,192,640]{2,1,0:T(8,128)(2,1)} async-done(((bf16[4,192,640]{2,1,0:T(8,128)(2,1)}), bf16[4,192,640]{2,1,0:T(8,128)(2,1)}, u32[]{:S(2)}, u32[]{:S(2)}) %all-to-all-start.7) | async-done | bytes 983072 | tf_op jit(solution)/shard_map/all_to_all | solution.py:211
  (170 shorter events, 165.2 us)
Async XLA Ops:
  0.0 15.7 %copy-start = (bf16[640,2560]{1,0:T(8,128)(2,1)S(1)}, bf16[640,2560]{1,0:T(8,128)(2,1)}, u32[]{:S(2)}) copy-start(bf16[640,2560]{1,0:T(8,128)(2,1)} %param.26) | copy-start | bytes 9830404
  0.0 7.7 %copy-start.17 = (bf16[192,640]{1,0:T(8,128)(2,1)S(1)}, bf16[192,640]{1,0:T(8,128)(2,1)}, u32[]{:S(2)}) copy-start(bf16[192,640]{1,0:T(8,128)(2,1)} %param.17) | copy-start | bytes 737284
  1.8 6.9 %copy-start.26 = (s32[4,48]{1,0:T(4,128)S(1)}, s32[4,48]{1,0:T(4,128)}, u32[]{:S(2)}) copy-start(s32[4,48]{1,0:T(4,128)} %param.24) | copy-start | bytes 2308
  16.6 6.1 %copy-start.21 = (s32[192,6]{0,1:T(8,128)S(1)}, s32[192,6]{0,1:T(8,128)}, u32[]{:S(2)}) copy-start(s32[192,6]{0,1:T(8,128)} %param.29) | copy-start | bytes 13828
  17.7 13.4 %copy-start.20 = (f32[2560]{0:T(1024)S(1)}, f32[2560]{0:T(1024)}, u32[]{:S(2)}) copy-start(f32[2560]{0:T(1024)} %param.27) | copy-start | bytes 30724
  17.7 29.3 %all-to-all-start = ((bf16[4,192,640]{2,1,0:T(8,128)(2,1)}), bf16[4,192,640]{2,1,0:T(8,128)(2,1)S(1)}, u32[]{:S(2)}, u32[]{:S(2)}) async-start(bf16[4,192,640]{2,1,0:T(8,128)(2,1)} %bitcast.228), calls=%async_computation | async-start | bytes 1966080 | tf_op jit(solution)/shard_map/all_to_all | solution.py:132
  78.6 35.1 %all-to-all-start.4 = ((bf16[8,96,1600]{2,1,0:T(8,128)(2,1)}), bf16[8,96,1600]{2,1,0:T(8,128)(2,1)}, u32[]{:S(2)}, u32[]{:S(2)}) async-start(bf16[8,96,1600]{2,1,0:T(8,128)(2,1)} %convolution_convert_fusion.3), calls=%async_computation.4 | async-start | bytes 5111808 | tf_op jit(solution)/shard_map/all_to_all | solution.py:158
  113.7 38.7 %all-to-all-start.1 = ((bf16[8,96,1600]{2,1,0:T(8,128)(2,1)}), bf16[8,96,1600]{2,1,0:T(8,128)(2,1)}, u32[]{:S(2)}, u32[]{:S(2)}) async-start(bf16[8,96,1600]{2,1,0:T(8,128)(2,1)} %convolution_convert_fusion.4), calls=%async_computation.1 | async-start | bytes 5111808 | tf_op jit(solution)/shard_map/all_to_all | solution.py:158
  121.2 13.4 %collective-permute-start.2 = (bf16[1,768,320]{1,2,0:T(8,128)(2,1)S(1)}, bf16[1,768,320]{1,2,0:T(8,128)(2,1)}, u32[]{:S(2)}, u32[]{:S(2)}) collective-permute-start(bf16[1,768,320]{1,2,0:T(8,128)(2,1)S(1)} %copy.207), channel_id=1, source_target_pairs={{0,1},{1,0},{2,3},{3,2},{4,5},{5,4},{6,7},{7,6},{8,9},{9,8},{10,11... | collective-permute-start | bytes 1474568 | tf_op jit(solution)/shard_map/ppermute | solution.py:18
  139.6 45.2 %collective-permute-start.3 = (bf16[2,768,320]{1,2,0:T(8,128)(2,1)}, bf16[2,768,320]{1,2,0:T(8,128)(2,1)}, u32[]{:S(2)}, u32[]{:S(2)}) collective-permute-start(bf16[2,768,320]{1,2,0:T(8,128)(2,1)} %copy.210), channel_id=1, source_target_pairs={{0,2},{1,3},{2,0},{3,1},{4,6},{5,7},{6,4},{7,5},{8,10},{9,11},{10,... | collective-permute-start | bytes 2949128 | tf_op jit(solution)/shard_map/ppermute | solution.py:18
  153.8 68.7 %collective-permute-start = (bf16[1,768,320]{1,2,0:T(8,128)(2,1)S(1)}, bf16[1,768,320]{1,2,0:T(8,128)(2,1)}, u32[]{:S(2)}, u32[]{:S(2)}) collective-permute-start(bf16[1,768,320]{1,2,0:T(8,128)(2,1)S(1)} %copy.195), channel_id=1, source_target_pairs={{0,1},{1,0},{2,3},{3,2},{4,5},{5,4},{6,7},{7,6},{8,9},{9,8},{10,11... | collective-permute-start | bytes 1474568 | tf_op jit(solution)/shard_map/ppermute | solution.py:18
  187.3 5.8 %copy-start.23 = (bf16[2,384,2560]{2,1,0:T(8,128)(2,1)S(1)}, bf16[2,384,2560]{2,1,0:T(8,128)(2,1)}, u32[]{:S(2)}) copy-start(bf16[2,384,2560]{2,1,0:T(8,128)(2,1)} %param.31) | copy-start | bytes 11796484
  217.7 124.7 %all-to-all-start.5 = ((bf16[4,768,320]{1,2,0:T(8,128)(2,1)}), bf16[4,768,320]{1,2,0:T(8,128)(2,1)}, u32[]{:S(2)}, u32[]{:S(2)}) async-start(bf16[4,768,320]{1,2,0:T(8,128)(2,1)} %bitcast.239), calls=%async_computation.5 | async-start | bytes 3932160 | tf_op jit(solution)/shard_map/all_to_all | solution.py:172
  227.6 82.9 %collective-permute-start.1 = (bf16[2,768,320]{1,2,0:T(8,128)(2,1)}, bf16[2,768,320]{1,2,0:T(8,128)(2,1)}, u32[]{:S(2)}, u32[]{:S(2)}) collective-permute-start(bf16[2,768,320]{1,2,0:T(8,128)(2,1)} %copy.198), channel_id=1, source_target_pairs={{0,2},{1,3},{2,0},{3,1},{4,6},{5,7},{6,4},{7,5},{8,10},{9,11},{10,... | collective-permute-start | bytes 2949128 | tf_op jit(solution)/shard_map/ppermute | solution.py:18
  233.1 6.1 %copy-start.3 = (bf16[1,2560,2,384]{3,1,2,0:T(8,128)(2,1)}, bf16[1,2560,2,384]{3,1,2,0:T(8,128)(2,1)S(1)}, u32[]{:S(2)}) copy-start(bf16[1,2560,2,384]{3,1,2,0:T(8,128)(2,1)S(1)} %copy.194) | copy-start | bytes 11796484
  233.3 79.5 %copy-start.7 = (bf16[2,768,320]{2,1,0:T(8,128)(2,1)S(1)}, bf16[2,768,320]{2,1,0:T(8,128)(2,1)}, u32[]{:S(2)}) copy-start(bf16[2,768,320]{2,1,0:T(8,128)(2,1)} %maximum_select_fusion.2) | copy-start | bytes 2949124
  312.9 5.1 %copy-start.24 = (bf16[2,384,2560]{2,1,0:T(8,128)(2,1)S(1)}, bf16[2,384,2560]{2,1,0:T(8,128)(2,1)}, u32[]{:S(2)}) copy-start(bf16[2,384,2560]{2,1,0:T(8,128)(2,1)} %param.31) | copy-start | bytes 11796484
  342.3 49.5 %all-to-all-start.2 = ((bf16[4,768,320]{1,2,0:T(8,128)(2,1)}), bf16[4,768,320]{1,2,0:T(8,128)(2,1)}, u32[]{:S(2)}, u32[]{:S(2)}) async-start(bf16[4,768,320]{1,2,0:T(8,128)(2,1)} %bitcast.241), calls=%async_computation.2 | async-start | bytes 3932160 | tf_op jit(solution)/shard_map/all_to_all | solution.py:172
  391.8 35.3 %all-to-all-start.6 = ((bf16[8,96,1600]{2,1,0:T(8,128)(2,1)}), bf16[8,96,1600]{2,1,0:T(8,128)(2,1)}, u32[]{:S(2)}, u32[]{:S(2)}) async-start(bf16[8,96,1600]{2,1,0:T(8,128)(2,1)} %pad_maximum_fusion.1), calls=%async_computation.6 | async-start | bytes 5111808 | tf_op jit(solution)/shard_map/all_to_all | solution.py:181
  415.3 17.6 %copy-start.19 = (f32[192,2,384]{2,0,1:T(8,128)S(1)}, f32[192,2,384]{2,0,1:T(8,128)}, u32[]{:S(2)}) copy-start(f32[192,2,384]{2,0,1:T(8,128)} %fusion.2) | copy-start | bytes 1769476
  427.1 36.0 %all-to-all-start.3 = ((bf16[8,96,1600]{2,1,0:T(8,128)(2,1)}), bf16[8,96,1600]{2,1,0:T(8,128)(2,1)}, u32[]{:S(2)}, u32[]{:S(2)}) async-start(bf16[8,96,1600]{2,1,0:T(8,128)(2,1)} %pad_maximum_fusion), calls=%async_computation.3 | async-start | bytes 5111808 | tf_op jit(solution)/shard_map/all_to_all | solution.py:181
  450.2 15.5 %copy-start.11 = (bf16[192,8,2,96]{3,0,1,2:T(8,128)(2,1)S(1)}, bf16[192,8,2,96]{3,0,1,2:T(8,128)(2,1)}, u32[]{:S(2)}) copy-start(bf16[192,8,2,96]{3,0,1,2:T(8,128)(2,1)} %copy-done.10) | copy-start | bytes 1769476
  473.5 33.8 %copy-start.1 = (bf16[640,2560]{1,0:T(8,128)(2,1)S(1)}, bf16[640,2560]{1,0:T(8,128)(2,1)}, u32[]{:S(2)}) copy-start(bf16[640,2560]{1,0:T(8,128)(2,1)} %param.26) | copy-start | bytes 9830404
  474.8 29.3 %all-to-all-start.7 = ((bf16[4,192,640]{2,1,0:T(8,128)(2,1)}), bf16[4,192,640]{2,1,0:T(8,128)(2,1)}, u32[]{:S(2)}, u32[]{:S(2)}) async-start(bf16[4,192,640]{2,1,0:T(8,128)(2,1)} %maximum_bitcast_fusion), calls=%async_computation.7 | async-start | bytes 1966080 | tf_op jit(solution)/shard_map/all_to_all | solution.py:211
  (15 other events, 39.4 us)
